TPU v7x, 256 devices: a whole 4x4x8 slice. The times are simulated.
256 devices in a mesh: section: 2 (over core), tok: 32 (over z, y), rep: 4 (over x).
Axes of the slice: x: 4, y: 4, z: 8, core: 2. Of those that a mesh axis runs over, the one named last changes fastest.
Arguments:
- inputs: bfloat16 [2, 4096, 1024], P(None, 'tok')
- segment_ids: int32 [2, 4096], replicated, may hold values from 0 to 7, as said below
- picks: int32 [2, 4096, 2], P(None, 'tok'), may hold values from 0 to 15, all different within a row; in each aligned block of 128 rows (0 to 127, 128 to 255, ..., all dimensions but the last counted through in order) at most 20 rows name the same one
- page_table: int32 [2, 32], replicated, may hold values from 0 to 31, each once within a row
- norm_gains: float32 [2, 2, 1024], P('section'), may hold values from 0.1 to 1.9
- attn_qkv: bfloat16 [2, 1024, 3, 1024], P('section', None, None, 'rep')
- attn_out: bfloat16 [2, 1024, 1024], P('section', 'rep'), may hold values from -0.1875 to 0.1875
- router: bfloat16 [2, 1024, 16], P('section')
- expert_in: bfloat16 [2, 32, 1024, 2, 1408], P('section', 'tok', None, None, 'rep'), may hold values from -0.1875 to 0.1875
- expert_out: bfloat16 [2, 32, 1408, 1024], P('section', 'tok', 'rep')
Outputs:
- layer_out: bfloat16 [2, 2, 4096, 1024], P('section', None, 'tok')
- kv_pages: bfloat16 [2, 2, 32, 128, 2, 1024], P('section', None, 'tok', None, None, 'rep')
Inputs may be any that keep to these rules, and one draw needn't show every extreme that they name: `picks`: within the tokens of one index of tok in one micro-batch, at most 20 tokens pick one expert, and some expert is picked by exactly 20. `segment_ids`: ids never fall along a micro-batch; every prompt has at least one token, a prompt spans at most 2048 tokens and one spans exactly 2048. `page_table`: each row is a permutation.
All inputs are finite; a program needn't handle non-finite values.
Results may differ from a plain program's by a relative error of at most 0.034.
Values may be sent and summed in bfloat16 or wider, within the bound.
No kernel may reach another device: no remote copies, remote signals or barrier semaphores. Data moves between devices by JAX's collectives and lax.ppermute only.
A program may use at most 128 MiB of HBM per device.

v0:
```python
import jax
import jax.numpy as jnp
from jax import lax
from jax.sharding import PartitionSpec as P

HEAD_DIM = 64
TOP = 2
PAGE = 128
CAP = 20
NEG_FILL = -1e30


def shifted(value, axis, steps):
    count = lax.axis_size(axis)
    first, last = (max(0, -steps), min(count, count - steps))
    return lax.ppermute(value, axis, [(source, source + steps) for source in range(first, last)])


def rms_scale(values, gains):
    return values * lax.rsqrt(jnp.mean(values * values, axis=-1, keepdims=True) + 1e-06) * gains


def attend(carry, queries, keys_vals, seg_query, pos_query, seg_key, pos_key):
    run_max, run_sum, run_acc = carry
    heads_here = run_acc.shape[0]
    head_size = run_acc.shape[2]
    rows_key = keys_vals.shape[0]
    key_part = keys_vals[:, 0].reshape(rows_key, heads_here, head_size)
    val_part = keys_vals[:, 1].reshape(rows_key, heads_here, head_size).astype(jnp.float32)
    scores = jnp.einsum(
        "thd,nhd->htn", queries, key_part, preferred_element_type=jnp.float32
    ) * head_size ** (-0.5)
    visible = (seg_query[:, None] == seg_key[None, :]) & (pos_query[:, None] >= pos_key[None, :])
    masked = jnp.where(visible[None], scores, NEG_FILL)
    new_max = jnp.maximum(run_max, jnp.max(masked, axis=-1))
    weights = jnp.where(visible[None], jnp.exp(masked - new_max[..., None]), 0.0)
    decay = jnp.exp(run_max - new_max)
    run_sum = run_sum * decay + jnp.sum(weights, axis=-1)
    run_acc = run_acc * decay[..., None] + jnp.einsum(
        "htn,nhd->htd", weights, val_part, precision=lax.Precision.HIGHEST
    )
    return (new_max, run_sum, run_acc)


def place_pages(pages, keys_vals, table_row, tok_index):
    rows_here = keys_vals.shape[0]
    blocks_dev = pages.shape[0]
    page_rows = pages.shape[1]
    block_ids = jnp.arange(table_row.shape[0], dtype=jnp.int32)
    wanted = tok_index * blocks_dev + 0
    source = jnp.sum(jnp.where(table_row == wanted, block_ids, 0))
    offset = source * page_rows
    inside = (offset >= 0) & (offset + page_rows <= rows_here)
    block = lax.dynamic_slice_in_dim(
        keys_vals, jnp.clip(offset, 0, rows_here - page_rows), page_rows, 0
    )
    updated = [jnp.where(inside, block, pages[0])]
    return jnp.stack(updated)


def one_layer(layer_in, seg_all, table_row, pick_rows, gains, w_qkv, w_out, w_router, w_in, w_down):
    tok_index = lax.axis_index("tok")
    tok_count = lax.axis_size("tok")
    tok_rows = layer_in.shape[0]
    width = layer_in.shape[1]
    col_width = w_qkv.shape[1] // 3
    head_count = col_width // HEAD_DIM
    experts_all = w_router.shape[1]
    local_pieces = w_in.shape[0]
    split_count = local_pieces * tok_count // experts_all
    blocks_dev = tok_rows // PAGE
    row_ids = jnp.arange(tok_rows, dtype=jnp.int32)
    pos_query = tok_index * tok_rows + row_ids
    seg_query = lax.dynamic_slice_in_dim(seg_all, tok_index * tok_rows, tok_rows)
    resid = layer_in.astype(jnp.float32)
    normed = rms_scale(resid, gains[0]).astype(jnp.bfloat16)
    projected = jnp.dot(normed, w_qkv, preferred_element_type=jnp.float32).astype(jnp.bfloat16)
    projected = projected.reshape(tok_rows, 3, col_width)
    queries = projected[:, 0].reshape(tok_rows, head_count, HEAD_DIM)
    keys_vals = projected[:, 1:]
    soft_init = (
        jnp.full((head_count, tok_rows), NEG_FILL, jnp.float32),
        jnp.zeros((head_count, tok_rows), jnp.float32),
        jnp.zeros((head_count, tok_rows, HEAD_DIM), jnp.float32),
    )
    empty_pages = jnp.zeros((blocks_dev, PAGE, 2, col_width), jnp.bfloat16)
    piece = lax.all_gather(keys_vals, "tok", axis=0, tiled=True)
    rows_key = piece.shape[0]
    step_rows = 1024
    while rows_key % step_rows != 0:
        step_rows = step_rows // 2
    turns = rows_key // step_rows

    def key_block(index, soft_now):
        start = index * step_rows
        block = lax.dynamic_slice_in_dim(piece, start, step_rows, 0)
        seg_key = lax.dynamic_slice_in_dim(seg_all, start, step_rows)
        pos_key = start + jnp.arange(step_rows, dtype=jnp.int32)
        return attend(soft_now, queries, block, seg_query, pos_query, seg_key, pos_key)

    soft_next = lax.fori_loop(0, turns, key_block, soft_init)
    pages = place_pages(empty_pages, piece, table_row, tok_index)
    run_max, run_sum, run_acc = soft_next
    context = (
        (run_acc / run_sum[..., None])
        .transpose(1, 0, 2)
        .reshape(tok_rows, col_width)
        .astype(jnp.bfloat16)
    )
    attn_part = jnp.dot(context, w_out, preferred_element_type=jnp.float32)
    mid = resid + lax.psum(attn_part, "rep")
    normed_mid = rms_scale(mid, gains[1]).astype(jnp.bfloat16)
    logits = jnp.dot(normed_mid, w_router, preferred_element_type=jnp.float32)
    expert_ids = jnp.arange(experts_all, dtype=jnp.int32)
    chosen = (pick_rows[:, :, None] == expert_ids[None, None, :]).astype(jnp.int32)
    picked_logit = jnp.sum(chosen.astype(jnp.float32) * logits[:, None, :], axis=-1)
    top_logit = jnp.max(picked_logit, axis=-1, keepdims=True)
    raised = jnp.exp(picked_logit - top_logit)
    gate_vals = raised / jnp.sum(raised, axis=-1, keepdims=True)
    ordered = chosen.transpose(1, 0, 2).reshape(TOP * tok_rows, experts_all)
    slot_of = jnp.sum((jnp.cumsum(ordered, axis=0) - 1) * ordered, axis=-1)
    flat_slot = pick_rows.T.reshape(TOP * tok_rows) * CAP + slot_of
    slot_ids = jnp.arange(experts_all * CAP, dtype=jnp.int32)
    hits = (flat_slot[:, None] == slot_ids[None, :]).astype(jnp.int32)
    hits = jnp.sum(hits.reshape(TOP, tok_rows, experts_all * CAP), axis=0).astype(jnp.bfloat16)
    dispatch = lax.dot_general(
        hits, normed_mid, (((0,), (0,)), ((), ())), preferred_element_type=jnp.float32
    ).astype(jnp.bfloat16)
    copies = jnp.broadcast_to(
        dispatch.reshape(experts_all, 1, CAP, width), (experts_all, split_count, CAP, width)
    )
    copies = copies.reshape(tok_count, local_pieces, CAP, width)
    act = jnp.einsum(
        "secd,edgf->secgf",
        lax.all_to_all(copies, "tok", split_axis=0, concat_axis=0, tiled=True),
        w_in,
        preferred_element_type=jnp.float32,
    )
    hidden = (jax.nn.gelu(act[..., 0, :]) * act[..., 1, :]).astype(jnp.bfloat16)
    returned = lax.all_to_all(
        jnp.einsum("secf,efd->secd", hidden, w_down, preferred_element_type=jnp.float32).astype(
            jnp.bfloat16
        ),
        "tok",
        split_axis=0,
        concat_axis=0,
        tiled=True,
    )
    summed = jnp.sum(
        returned.reshape(experts_all, split_count, CAP, width).astype(jnp.float32), axis=1
    )
    summed = summed.reshape(experts_all * CAP, width)
    gathered = jnp.take(summed, flat_slot, axis=0).reshape(TOP, tok_rows, width)
    expert_local = jnp.sum(gate_vals.T[:, :, None] * gathered, axis=0)
    expert_total = lax.psum(expert_local, "rep")
    layer_result = (mid + expert_total).astype(jnp.bfloat16)
    return (layer_result, pages)


def per_device(
    inputs,
    segment_ids,
    picks,
    page_table,
    norm_gains,
    attn_qkv,
    attn_out,
    router,
    expert_in,
    expert_out,
):
    section_index = lax.axis_index("section")
    is_first = section_index == 0
    width = inputs.shape[2]
    own = (
        norm_gains[0],
        attn_qkv[0].reshape(width, -1),
        attn_out[0],
        router[0],
        expert_in[0],
        expert_out[0],
    )
    swap = [(0, 1), (1, 0)]
    other = tuple((lax.ppermute(w, "section", swap) for w in own))
    weights_of = [
        tuple((jnp.where(is_first, a, b) for a, b in zip(own, other))),
        tuple((jnp.where(is_first, b, a) for a, b in zip(own, other))),
    ]
    micro = section_index
    hidden = lax.dynamic_index_in_dim(inputs, micro, 0, keepdims=False)
    seg_all = lax.dynamic_index_in_dim(segment_ids, micro, 0, keepdims=False)
    table_row = lax.dynamic_index_in_dim(page_table, micro, 0, keepdims=False)
    pick_rows = lax.dynamic_index_in_dim(picks, micro, 0, keepdims=False)
    results = []
    for layer in range(2):
        hidden, pages = one_layer(hidden, seg_all, table_row, pick_rows, *weights_of[layer])
        results.append((hidden, pages))
    (res0, pages0), (res1, pages1) = results
    got0 = lax.ppermute(res0, "section", [(1, 0)])
    gotp0 = lax.ppermute(pages0, "section", [(1, 0)])
    got1 = lax.ppermute(res1, "section", [(0, 1)])
    gotp1 = lax.ppermute(pages1, "section", [(0, 1)])
    outputs = jnp.where(is_first, jnp.stack([res0, got0]), jnp.stack([got1, res1]))
    page_out = jnp.where(is_first, jnp.stack([pages0, gotp0]), jnp.stack([gotp1, pages1]))
    return (outputs[None], page_out[None])


def solution(mesh):
    return jax.shard_map(
        per_device,
        mesh=mesh,
        in_specs=(
            P(None, "tok", None),
            P(),
            P(None, "tok", None),
            P(),
            P("section", None, None),
            P("section", None, None, "rep"),
            P("section", "rep", None),
            P("section", None, None),
            P("section", "tok", None, None, "rep"),
            P("section", "tok", "rep", None),
        ),
        out_specs=(P("section", None, "tok", None), P("section", None, "tok", None, None, "rep")),
        check_vma=False,
    )
```

profile of v0, /device:TPU:1, one launch (start us, length us, event | category | flops | bytes accessed | tf_op | source)
XLA Modules:
  0.0 634.5 jit_solution(9774270104577038417)
XLA Ops:
  9.0 3.3 collective-permute-start.1
  12.6 2.9 collective-permute-done
  19.5 79.9 %all-gather.3.cloned.1.call-done = bf16[4096,2,256]{0,2,1:T(8,128)(2,1)} async-done(((bf16[128,2,256]{0,2,1:T(8,128)(2,1)}), bf16[4096,2,256]{0,2,1:T(8,128)(2,1)}) %all-gather.3.cloned.1.call-update) | async-done | bytes 4194320 | tf_op jit(solution)/shard_map/all_gather | solution.py:87
  99.4 17.1 %while.36 = (s32[]{:T(128)}, f32[4,128]{1,0:T(4,128)S(1)}, f32[4,128]{1,0:T(4,128)S(1)}, f32[4,128,64]{1,2,0:T(8,128)S(1)}, s32[128]{0:T(128)S(1)}, /*index=5*/s...) while((s32[]{:T(128)}, f32[4,128]{1,0:T(4,128)S(1)}, ...), condition=%wide.region_4.5_spmd.clone, body=%wide.region_1.4_spmd.clone.sunk | while | flops 476548736 | bytes 10344167 | solution.py:101
  118.0 49.1 %all-reduce.5.cloned.1.call-done = f32[128,1024]{1,0:T(8,128)} async-done(((f32[128,1024]{1,0:T(8,128)}), f32[128,1024]{1,0:T(8,128)}) %all-reduce.5.cloned.1.call-update) | async-done | bytes 524304 | tf_op jit(solution)/shard_map/psum | solution.py:111
  171.5 9.7 %all-to-all-start = ((bf16[32,1,20,1024]{3,2,1,0:T(8,128)(2,1)}), bf16[32,1,20,1024]{3,2,1,0:T(8,128)(2,1)S(1)}, u32[]{:S(2)}, u32[]{:S(2)}) async-start(bf16[32,1,20,1024]{3,2,1,0:T(8,128)(2,1)} %bitcast.29), calls=%async_computation | async-start | bytes 3145728 | tf_op jit(solution)/shard_map/all_to_all | solution.py:135
  181.2 3.2 collective-permute-start.5
  184.7 2.9 collective-permute-done.5
  187.6 28.6 %all-to-all-done = bf16[32,1,20,1024]{3,2,1,0:T(8,128)(2,1)S(1)} async-done(((bf16[32,1,20,1024]{3,2,1,0:T(8,128)(2,1)}), bf16[32,1,20,1024]{3,2,1,0:T(8,128)(2,1)S(1)}, u32[]{:S(2)}, u32[]{:S(2)}) %all-to-all-start) | async-done | bytes 1310752 | tf_op jit(solution)/shard_map/all_to_all | solution.py:135
  216.2 3.6 convolution_bitcast_fusion.1
  219.8 2.3 fusion.42
  224.1 7.5 %all-to-all-start.1 = ((bf16[32,1,20,1024]{3,2,1,0:T(8,128)(2,1)}), bf16[32,1,20,1024]{3,2,1,0:T(8,128)(2,1)S(1)}, u32[]{:S(2)}, u32[]{:S(2)}) async-start(bf16[32,1,20,1024]{3,2,1,0:T(8,128)(2,1)} %copy.59), calls=%async_computation.1 | async-start | bytes 3145728 | tf_op jit(solution)/shard_map/all_to_all | solution.py:140
  231.7 2.9 collective-permute-start.3
  235.6 31.5 %all-to-all-done.1 = bf16[32,1,20,1024]{3,2,1,0:T(8,128)(2,1)S(1)} async-done(((bf16[32,1,20,1024]{3,2,1,0:T(8,128)(2,1)}), bf16[32,1,20,1024]{3,2,1,0:T(8,128)(2,1)S(1)}, u32[]{:S(2)}, u32[]{:S(2)}) %all-to-all-start.1) | async-done | bytes 1310752 | tf_op jit(solution)/shard_map/all_to_all | solution.py:140
  269.9 47.1 %all-reduce.7.cloned.1.call-done = f32[128,1024]{1,0:T(8,128)} async-done(((f32[128,1024]{1,0:T(8,128)}), f32[128,1024]{1,0:T(8,128)}) %all-reduce.7.cloned.1.call-update) | async-done | bytes 524304 | tf_op jit(solution)/shard_map/psum | solution.py:155
  319.9 84.1 %all-gather.5.cloned.1.call-done = bf16[4096,2,256]{0,2,1:T(8,128)(2,1)} async-done(((bf16[128,2,256]{0,2,1:T(8,128)(2,1)}), bf16[4096,2,256]{0,2,1:T(8,128)(2,1)}) %all-gather.5.cloned.1.call-update) | async-done | bytes 4194320 | tf_op jit(solution)/shard_map/all_gather | solution.py:87
  404.0 17.1 %while.37 = (s32[]{:T(128)}, f32[4,128]{1,0:T(4,128)S(1)}, f32[4,128]{1,0:T(4,128)S(1)}, f32[4,128,64]{1,2,0:T(8,128)S(1)}, s32[128]{0:T(128)S(1)}, /*index=5*/s...) while((s32[]{:T(128)}, f32[4,128]{1,0:T(4,128)S(1)}, ...), condition=%wide.region_21.23_spmd.clone, body=%wide.region_18.22_spmd.clone.sunk | while | flops 476548736 | bytes 10344167 | solution.py:101
  422.3 49.5 %all-reduce.9.cloned.1.call-done = f32[128,1024]{1,0:T(8,128)} async-done(((f32[128,1024]{1,0:T(8,128)}), f32[128,1024]{1,0:T(8,128)}) %all-reduce.9.cloned.1.call-update) | async-done | bytes 524304 | tf_op jit(solution)/shard_map/psum | solution.py:111
  474.8 45.7 %all_to_all.20 = bf16[32,1,20,1024]{3,2,1,0:T(8,128)(2,1)S(1)} all-to-all(bf16[32,1,20,1024]{3,2,1,0:T(8,128)(2,1)S(1)} %bitcast.258), channel_id=1, replica_groups=mesh['section'=2,'tok'=32,'rep'=4] {'tok'}, dimensions={0} | all-to-all | bytes 2621440 | tf_op jit(solution)/shard_map/all_to_all | solution.py:135
  525.3 6.1 all-to-all-start.3
  531.7 31.8 %all-to-all-done.3 = bf16[32,1,20,1024]{3,2,1,0:T(8,128)(2,1)S(1)} async-done(((bf16[32,1,20,1024]{3,2,1,0:T(8,128)(2,1)}), bf16[32,1,20,1024]{3,2,1,0:T(8,128)(2,1)S(1)}, u32[]{:S(2)}, u32[]{:S(2)}) %all-to-all-start.3) | async-done | bytes 1310752 | tf_op jit(solution)/shard_map/all_to_all | solution.py:140
  568.6 9.9 %collective-permute-start.8 = (bf16[1,128,2,256]{1,3,2,0:T(8,128)(2,1)S(1)}, bf16[1,128,2,256]{1,3,2,0:T(8,128)(2,1)S(1)}, u32[]{:S(2)}, u32[]{:S(2)}) collective-permute-start(bf16[1,128,2,256]{1,3,2,0:T(8,128)(2,1)S(1)} %get-tuple-element.462), channel_id=1, source_target_pairs={{128,0},{129,1},{130,2},{131,3},{132,4},{133,5},{134,6},{135,7},{1... | collective-permute-start | bytes 393224 | tf_op jit(solution)/shard_map/ppermute | solution.py:200
  579.8 37.5 %all-reduce.11.cloned.1.call-done = f32[128,1024]{1,0:T(8,128)} async-done(((f32[128,1024]{1,0:T(8,128)}), f32[128,1024]{1,0:T(8,128)}) %all-reduce.11.cloned.1.call-update) | async-done | bytes 524304 | tf_op jit(solution)/shard_map/psum | solution.py:155
  622.1 3.7 collective-permute-done.9
  (232 shorter events, 75.8 us)
Async XLA Ops:
  7.2 92.2 %all-gather.3.cloned.1.call-start = ((), (), s32[]{:S(2)}) async-start(), calls=%async_computation.4 | async-start | bytes 4325376 | tf_op jit(solution)/shard_map/all_gather | solution.py:87
  9.0 6.5 %collective-permute-start.1 = (bf16[1024,768]{0,1:T(8,128)(2,1)S(1)}, bf16[1024,768]{0,1:T(8,128)(2,1)}, u32[]{:S(2)}, u32[]{:S(2)}) collective-permute-start(bf16[1024,768]{0,1:T(8,128)(2,1)S(1)} %bitcast.264), channel_id=1, source_target_pairs={{0,128},{128,0},{1,129},{129,1},{2,130},{130,2},{3,131},{131,3},{4... | collective-permute-start | bytes 4718600 | tf_op jit(solution)/shard_map/ppermute | solution.py:184
  12.3 3.2 collective-permute-start
  18.6 148.6 %all-reduce.5.cloned.1.call-start = ((), (), s32[]{:S(2)}) async-start(), calls=%async_computation.5 | async-start | bytes 1048576 | tf_op jit(solution)/shard_map/psum | solution.py:111
  18.6 97.9 %collective-permute-start.2 = (bf16[256,1024]{1,0:T(8,128)(2,1)S(1)}, bf16[256,1024]{1,0:T(8,128)(2,1)S(1)}, u32[]{:S(2)}, u32[]{:S(2)}) collective-permute-start(bf16[256,1024]{1,0:T(8,128)(2,1)S(1)} %bitcast.263), channel_id=1, source_target_pairs={{0,128},{128,0},{1,129},{129,1},{2,130},{130,2},{3,131},{131,3},{4... | collective-permute-start | bytes 1572872 | tf_op jit(solution)/shard_map/ppermute | solution.py:184
  116.6 51.8 %copy-start.8 = (bf16[256,1024]{1,0:T(8,128)(2,1)}, bf16[256,1024]{1,0:T(8,128)(2,1)S(1)}, u32[]{:S(2)}) copy-start(bf16[256,1024]{1,0:T(8,128)(2,1)S(1)} %collective-permute-done.2) | copy-start | bytes 1572868
  171.5 44.8 %all-to-all-start = ((bf16[32,1,20,1024]{3,2,1,0:T(8,128)(2,1)}), bf16[32,1,20,1024]{3,2,1,0:T(8,128)(2,1)S(1)}, u32[]{:S(2)}, u32[]{:S(2)}) async-start(bf16[32,1,20,1024]{3,2,1,0:T(8,128)(2,1)} %bitcast.29), calls=%async_computation | async-start | bytes 3145728 | tf_op jit(solution)/shard_map/all_to_all | solution.py:135
  181.2 6.4 %collective-permute-start.5 = (bf16[1,1024,2,352]{1,3,2,0:T(8,128)(2,1)}, bf16[1,1024,2,352]{1,3,2,0:T(8,128)(2,1)}, u32[]{:S(2)}, u32[]{:S(2)}) collective-permute-start(bf16[1,1024,2,352]{1,3,2,0:T(8,128)(2,1)} %bitcast.285), channel_id=1, source_target_pairs={{0,128},{128,0},{1,129},{129,1},{2,130},{130,2},{3,131},{131,3},{4... | collective-permute-start | bytes 4325384 | tf_op jit(solution)/shard_map/ppermute | solution.py:184
  184.4 35.4 %collective-permute-start.4 = (bf16[1,352,1024]{2,1,0:T(8,128)(2,1)S(1)}, bf16[1,352,1024]{2,1,0:T(8,128)(2,1)}, u32[]{:S(2)}, u32[]{:S(2)}) collective-permute-start(bf16[1,352,1024]{2,1,0:T(8,128)(2,1)S(1)} %bitcast.286), channel_id=1, source_target_pairs={{0,128},{128,0},{1,129},{129,1},{2,130},{130,2},{3,131},{131,3},{4... | collective-permute-start | bytes 2162696 | tf_op jit(solution)/shard_map/ppermute | solution.py:184
  224.1 43.1 %all-to-all-start.1 = ((bf16[32,1,20,1024]{3,2,1,0:T(8,128)(2,1)}), bf16[32,1,20,1024]{3,2,1,0:T(8,128)(2,1)S(1)}, u32[]{:S(2)}, u32[]{:S(2)}) async-start(bf16[32,1,20,1024]{3,2,1,0:T(8,128)(2,1)} %copy.59), calls=%async_computation.1 | async-start | bytes 3145728 | tf_op jit(solution)/shard_map/all_to_all | solution.py:140
  231.6 85.4 %all-reduce.7.cloned.1.call-start = ((), (), s32[]{:S(2)}) async-start(), calls=%async_computation.6 | async-start | bytes 1048576 | tf_op jit(solution)/shard_map/psum | solution.py:155
  231.7 3.7 collective-permute-start.3
  268.7 48.3 %copy-start.3 = (f32[128,1024]{1,0:T(8,128)S(1)}, f32[128,1024]{1,0:T(8,128)}, u32[]{:S(2)}) copy-start(f32[128,1024]{1,0:T(8,128)} %all-reduce.5.cloned.1.call-done) | copy-start | bytes 1572868
  268.8 48.3 %copy-start.5 = (bf16[2,128,1024]{2,1,0:T(8,128)(2,1)S(1)}, bf16[2,128,1024]{2,1,0:T(8,128)(2,1)}, u32[]{:S(2)}) copy-start(bf16[2,128,1024]{2,1,0:T(8,128)(2,1)} %param.16) | copy-start | bytes 1572868
  268.9 49.3 %copy-start.11 = (bf16[1,1024,3,256]{1,3,2,0:T(8,128)(2,1)S(1)}, bf16[1,1024,3,256]{1,3,2,0:T(8,128)(2,1)}, u32[]{:S(2)}) copy-start(bf16[1,1024,3,256]{1,3,2,0:T(8,128)(2,1)} %copy-done.10) | copy-start | bytes 4718596
  269.9 134.2 %all-gather.5.cloned.1.call-start = ((), (), s32[]{:S(2)}) async-start(), calls=%async_computation.7 | async-start | bytes 4325376 | tf_op jit(solution)/shard_map/all_gather | solution.py:87
  319.8 152.0 %all-reduce.9.cloned.1.call-start = ((), (), s32[]{:S(2)}) async-start(), calls=%async_computation.8 | async-start | bytes 1048576 | tf_op jit(solution)/shard_map/psum | solution.py:111
  525.3 38.2 %all-to-all-start.3 = ((bf16[32,1,20,1024]{3,2,1,0:T(8,128)(2,1)}), bf16[32,1,20,1024]{3,2,1,0:T(8,128)(2,1)S(1)}, u32[]{:S(2)}, u32[]{:S(2)}) async-start(bf16[32,1,20,1024]{3,2,1,0:T(8,128)(2,1)} %copy.64), calls=%async_computation.3 | async-start | bytes 3145728 | tf_op jit(solution)/shard_map/all_to_all | solution.py:140
  531.4 85.8 %all-reduce.11.cloned.1.call-start = ((), (), s32[]{:S(2)}) async-start(), calls=%async_computation.9 | async-start | bytes 1048576 | tf_op jit(solution)/shard_map/psum | solution.py:155
  565.1 52.2 %copy-start.2 = (f32[128,1024]{1,0:T(8,128)S(1)}, f32[128,1024]{1,0:T(8,128)}, u32[]{:S(2)}) copy-start(f32[128,1024]{1,0:T(8,128)} %all-reduce.9.cloned.1.call-done) | copy-start | bytes 1572868
  568.6 53.5 %collective-permute-start.8 = (bf16[1,128,2,256]{1,3,2,0:T(8,128)(2,1)S(1)}, bf16[1,128,2,256]{1,3,2,0:T(8,128)(2,1)S(1)}, u32[]{:S(2)}, u32[]{:S(2)}) collective-permute-start(bf16[1,128,2,256]{1,3,2,0:T(8,128)(2,1)S(1)} %get-tuple-element.462), channel_id=1, source_target_pairs={{128,0},{129,1},{130,2},{131,3},{132,4},{133,5},{134,6},{135,7},{1... | collective-permute-start | bytes 393224 | tf_op jit(solution)/shard_map/ppermute | solution.py:200
  578.5 48.3 %collective-permute-start.6 = (bf16[128,1024]{1,0:T(8,128)(2,1)S(1)}, bf16[128,1024]{1,0:T(8,128)(2,1)S(1)}, u32[]{:S(2)}, u32[]{:S(2)}) collective-permute-start(bf16[128,1024]{1,0:T(8,128)(2,1)S(1)} %get-tuple-element.448), channel_id=1, source_target_pairs={{128,0},{129,1},{130,2},{131,3},{132,4},{133,5},{134,6},{135,7},{1... | collective-permute-start | bytes 786440 | tf_op jit(solution)/shard_map/ppermute | solution.py:199
  618.4 8.3 %collective-permute-start.7 = (bf16[128,1024]{1,0:T(8,128)(2,1)S(1)}, bf16[128,1024]{1,0:T(8,128)(2,1)S(1)}, u32[]{:S(2)}, u32[]{:S(2)}) collective-permute-start(bf16[128,1024]{1,0:T(8,128)(2,1)S(1)} %add_convert_fusion), channel_id=1, source_target_pairs={{0,128},{1,129},{2,130},{3,131},{4,132},{5,133},{6,134},{7,135},{8... | collective-permute-start | bytes 786440 | tf_op jit(solution)/shard_map/ppermute | solution.py:201
  620.8 5.0 collective-permute-start.9
  (14 other events, 151.4 us)
Sparse Core Ops, SparseCore 0:
  18.7 80.6 all-gather.2
  117.8 49.3 all-reduce.4
  270.0 46.9 all-reduce.6
  319.9 84.0 all-gather.4
  422.4 49.3 all-reduce.8
  566.3 50.8 all-reduce.10
where the time goes:
time: 636 us; the launch traced here: 634 us
  waiting for transfers between devices  450 us (71%)
  starting transfers between devices  47.2 us (7%)
  blocking collectives  45.7 us (7%)
  matrix products  30.8 us (5%)
  local copies, waits for them, and re-layouts  23.3 us (4%)
  other arithmetic  22 us (3%)
  between operations  15.4 us (2%)
    all_gather x2, waiting for transfers between devices, one_layer(): piece = lax.all_gather(keys_vals, 'tok', axis=0, tiled=True)  164 us
    psum x2, waiting for transfers between devices, one_layer(): mid = resid + lax.psum(attn_part, 'rep')  98.6 us
    psum x2, waiting for transfers between devices, one_layer(): expert_total = lax.psum(expert_local, 'rep')  84.6 us
    all_to_all x2, waiting for transfers between devices, one_layer(): lax.all_to_all(jnp.einsum('secf,efd->secd', hidden, w_down, preferred_ele...  63.3 us
    all_to_all x1, blocking collectives, one_layer(): lax.all_to_all(copies, 'tok', split_axis=0, concat_axis=0, tiled=True)  45.7 us
    all_to_all x1, waiting for transfers between devices, one_layer(): lax.all_to_all(copies, 'tok', split_axis=0, concat_axis=0, tiled=True)  28.6 us
    all_to_all x2, starting transfers between devices, one_layer(): lax.all_to_all(jnp.einsum('secf,efd->secd', hidden, w_down, preferred_ele...  13.6 us
  transfers between devices with their start and end apart: 19, of which 13 were waited for; matrix products, arithmetic and copies ran while one was open for 4% of the time, Pallas kernels for 0%

commit v1 on v0

--- a/solution.py
+++ b/solution.py
@@ -152,7 +152,8 @@
     summed = summed.reshape(experts_all * CAP, width)
     gathered = jnp.take(summed, flat_slot, axis=0).reshape(TOP, tok_rows, width)
     expert_local = jnp.sum(gate_vals.T[:, :, None] * gathered, axis=0)
-    expert_total = lax.psum(expert_local, "rep")
+    terms = lax.all_gather(expert_local, "rep", axis=0, tiled=False)
+    expert_total = terms.sum(axis=0)
     layer_result = (mid + expert_total).astype(jnp.bfloat16)
     return (layer_result, pages)
 

time: 636 us -> 607 us (0.954)
  waiting for transfers between devices: 450 us -> 421 us
    psum x2 -> x0, waiting for transfers between devices: 84.6 us -> none  [one_layer(): expert_total = lax.psum(expert_local, 'rep')]
    all_gather x0 -> x2, waiting for transfers between devices: none -> 58.6 us  [one_layer(): terms = lax.all_gather(expert_local, 'rep', axis=0, tiled=False)]
  transfers between devices with their start and end apart: 19 -> 19, of which waited for: 13 -> 13; matrix products, arithmetic and copies ran while one was open for 4% -> 5% of each run, Pallas kernels for 0% -> 0%
where the time goes in v1:
time: 607 us; the launch traced here: 606 us
  waiting for transfers between devices  421 us (69%)
  starting transfers between devices  46.3 us (8%)
  blocking collectives  45.7 us (8%)
  matrix products  30.6 us (5%)
  other arithmetic  23.6 us (4%)
  local copies, waits for them, and re-layouts  23.2 us (4%)
  between operations  15.5 us (3%)
    all_gather x2, waiting for transfers between devices, one_layer(): piece = lax.all_gather(keys_vals, 'tok', axis=0, tiled=True)  162 us
    psum x2, waiting for transfers between devices, one_layer(): mid = resid + lax.psum(attn_part, 'rep')  98.7 us
    all_to_all x2, waiting for transfers between devices, one_layer(): lax.all_to_all(jnp.einsum('secf,efd->secd', hidden, w_down, preferred_ele...  64.5 us
    all_gather x2, waiting for transfers between devices, one_layer(): terms = lax.all_gather(expert_local, 'rep', axis=0, tiled=False)  58.6 us
    all_to_all x1, blocking collectives, one_layer(): lax.all_to_all(copies, 'tok', split_axis=0, concat_axis=0, tiled=True)  45.7 us
    all_to_all x1, waiting for transfers between devices, one_layer(): lax.all_to_all(copies, 'tok', split_axis=0, concat_axis=0, tiled=True)  28.6 us
    all_to_all x2, starting transfers between devices, one_layer(): lax.all_to_all(jnp.einsum('secf,efd->secd', hidden, w_down, preferred_ele...  13.6 us
  transfers between devices with their start and end apart: 19, of which 13 were waited for; matrix products, arithmetic and copies ran while one was open for 5% of the time, Pallas kernels for 0%

profile of v1, /device:TPU:1, one launch (start us, length us, event | category | flops | bytes accessed | tf_op | source)
XLA Modules:
  0.0 606.0 jit_solution(3488729540491406978)
XLA Ops:
  9.0 3.3 collective-permute-start.1
  12.6 2.9 collective-permute-done
  15.5 2.1 fusion.48
  19.5 79.9 %all-gather.7.cloned.1.call-done = bf16[4096,2,256]{0,2,1:T(8,128)(2,1)} async-done(((bf16[128,2,256]{0,2,1:T(8,128)(2,1)}), bf16[4096,2,256]{0,2,1:T(8,128)(2,1)}) %all-gather.7.cloned.1.call-update) | async-done | bytes 4194320 | tf_op jit(solution)/shard_map/all_gather | solution.py:87
  99.4 17.1 %while.36 = (s32[]{:T(128)}, f32[4,128]{1,0:T(4,128)S(1)}, f32[4,128]{1,0:T(4,128)S(1)}, f32[4,128,64]{1,2,0:T(8,128)S(1)}, s32[128]{0:T(128)S(1)}, /*index=5*/s...) while((s32[]{:T(128)}, f32[4,128]{1,0:T(4,128)S(1)}, ...), condition=%wide.region_4.5_spmd.clone, body=%wide.region_1.4_spmd.clone.sunk | while | flops 476548736 | bytes 10344167 | solution.py:101
  118.1 49.1 %all-reduce.3.cloned.1.call-done = f32[128,1024]{1,0:T(8,128)} async-done(((f32[128,1024]{1,0:T(8,128)}), f32[128,1024]{1,0:T(8,128)}) %all-reduce.3.cloned.1.call-update) | async-done | bytes 524304 | tf_op jit(solution)/shard_map/psum | solution.py:111
  171.4 9.7 %all-to-all-start = ((bf16[32,1,20,1024]{3,2,1,0:T(8,128)(2,1)}), bf16[32,1,20,1024]{3,2,1,0:T(8,128)(2,1)S(1)}, u32[]{:S(2)}, u32[]{:S(2)}) async-start(bf16[32,1,20,1024]{3,2,1,0:T(8,128)(2,1)} %bitcast.29), calls=%async_computation | async-start | bytes 3145728 | tf_op jit(solution)/shard_map/all_to_all | solution.py:135
  181.1 3.2 collective-permute-start.5
  184.7 2.9 collective-permute-done.5
  187.6 28.6 %all-to-all-done = bf16[32,1,20,1024]{3,2,1,0:T(8,128)(2,1)S(1)} async-done(((bf16[32,1,20,1024]{3,2,1,0:T(8,128)(2,1)}), bf16[32,1,20,1024]{3,2,1,0:T(8,128)(2,1)S(1)}, u32[]{:S(2)}, u32[]{:S(2)}) %all-to-all-start) | async-done | bytes 1310752 | tf_op jit(solution)/shard_map/all_to_all | solution.py:135
  216.2 3.6 convolution_bitcast_fusion.1
  219.7 2.1 fusion.42
  223.8 7.5 %all-to-all-start.1 = ((bf16[32,1,20,1024]{3,2,1,0:T(8,128)(2,1)}), bf16[32,1,20,1024]{3,2,1,0:T(8,128)(2,1)S(1)}, u32[]{:S(2)}, u32[]{:S(2)}) async-start(bf16[32,1,20,1024]{3,2,1,0:T(8,128)(2,1)} %copy.59), calls=%async_computation.1 | async-start | bytes 3145728 | tf_op jit(solution)/shard_map/all_to_all | solution.py:140
  234.4 32.7 %all-to-all-done.1 = bf16[32,1,20,1024]{3,2,1,0:T(8,128)(2,1)S(1)} async-done(((bf16[32,1,20,1024]{3,2,1,0:T(8,128)(2,1)}), bf16[32,1,20,1024]{3,2,1,0:T(8,128)(2,1)S(1)}, u32[]{:S(2)}, u32[]{:S(2)}) %all-to-all-start.1) | async-done | bytes 1310752 | tf_op jit(solution)/shard_map/all_to_all | solution.py:140
  269.9 33.9 %all-gather.11.cloned.1.call-done = f32[512,1024]{1,0:T(8,128)} async-done(((f32[128,1024]{1,0:T(8,128)}), f32[512,1024]{1,0:T(8,128)}) %all-gather.11.cloned.1.call-update) | async-done | bytes 2097168 | tf_op jit(solution)/shard_map/all_gather | solution.py:155
  307.6 81.6 %all-gather.9.cloned.1.call-done = bf16[4096,2,256]{0,2,1:T(8,128)(2,1)} async-done(((bf16[128,2,256]{0,2,1:T(8,128)(2,1)}), bf16[4096,2,256]{0,2,1:T(8,128)(2,1)}) %all-gather.9.cloned.1.call-update) | async-done | bytes 4194320 | tf_op jit(solution)/shard_map/all_gather | solution.py:87
  389.2 17.1 %while.37 = (s32[]{:T(128)}, f32[4,128]{1,0:T(4,128)S(1)}, f32[4,128]{1,0:T(4,128)S(1)}, f32[4,128,64]{1,2,0:T(8,128)S(1)}, s32[128]{0:T(128)S(1)}, /*index=5*/s...) while((s32[]{:T(128)}, f32[4,128]{1,0:T(4,128)S(1)}, ...), condition=%wide.region_21.23_spmd.clone, body=%wide.region_18.22_spmd.clone.sunk | while | flops 476548736 | bytes 10344167 | solution.py:101
  407.5 49.5 %all-reduce.5.cloned.1.call-done = f32[128,1024]{1,0:T(8,128)} async-done(((f32[128,1024]{1,0:T(8,128)}), f32[128,1024]{1,0:T(8,128)}) %all-reduce.5.cloned.1.call-update) | async-done | bytes 524304 | tf_op jit(solution)/shard_map/psum | solution.py:111
  460.1 45.7 %all_to_all.20 = bf16[32,1,20,1024]{3,2,1,0:T(8,128)(2,1)S(1)} all-to-all(bf16[32,1,20,1024]{3,2,1,0:T(8,128)(2,1)S(1)} %bitcast.260), channel_id=1, replica_groups=mesh['section'=2,'tok'=32,'rep'=4] {'tok'}, dimensions={0} | all-to-all | bytes 2621440 | tf_op jit(solution)/shard_map/all_to_all | solution.py:135
  508.7 2.0 copy.64
  510.6 6.1 %all-to-all-start.3 = ((bf16[32,1,20,1024]{3,2,1,0:T(8,128)(2,1)}), bf16[32,1,20,1024]{3,2,1,0:T(8,128)(2,1)S(1)}, u32[]{:S(2)}, u32[]{:S(2)}) async-start(bf16[32,1,20,1024]{3,2,1,0:T(8,128)(2,1)} %copy.64), calls=%async_computation.3 | async-start | bytes 3145728 | tf_op jit(solution)/shard_map/all_to_all | solution.py:140
  517.0 31.8 %all-to-all-done.3 = bf16[32,1,20,1024]{3,2,1,0:T(8,128)(2,1)S(1)} async-done(((bf16[32,1,20,1024]{3,2,1,0:T(8,128)(2,1)}), bf16[32,1,20,1024]{3,2,1,0:T(8,128)(2,1)S(1)}, u32[]{:S(2)}, u32[]{:S(2)}) %all-to-all-start.3) | async-done | bytes 1310752 | tf_op jit(solution)/shard_map/all_to_all | solution.py:140
  553.9 9.9 %collective-permute-start.8 = (bf16[1,128,2,256]{1,3,2,0:T(8,128)(2,1)S(1)}, bf16[1,128,2,256]{1,3,2,0:T(8,128)(2,1)S(1)}, u32[]{:S(2)}, u32[]{:S(2)}) collective-permute-start(bf16[1,128,2,256]{1,3,2,0:T(8,128)(2,1)S(1)} %get-tuple-element.462), channel_id=1, source_target_pairs={{128,0},{129,1},{130,2},{131,3},{132,4},{133,5},{134,6},{135,7},{1... | collective-permute-start | bytes 393224 | tf_op jit(solution)/shard_map/ppermute | solution.py:201
  565.1 24.7 %all-gather.13.cloned.1.call-done = f32[512,1024]{1,0:T(8,128)} async-done(((f32[128,1024]{1,0:T(8,128)}), f32[512,1024]{1,0:T(8,128)}) %all-gather.13.cloned.1.call-update) | async-done | bytes 2097168 | tf_op jit(solution)/shard_map/all_gather | solution.py:155
  (238 shorter events, 77.1 us)
Async XLA Ops:
  7.2 92.2 %all-gather.7.cloned.1.call-start = ((), (), s32[]{:S(2)}) async-start(), calls=%async_computation.4 | async-start | bytes 4325376 | tf_op jit(solution)/shard_map/all_gather | solution.py:87
  9.0 6.5 %collective-permute-start.1 = (bf16[1024,768]{0,1:T(8,128)(2,1)S(1)}, bf16[1024,768]{0,1:T(8,128)(2,1)}, u32[]{:S(2)}, u32[]{:S(2)}) collective-permute-start(bf16[1024,768]{0,1:T(8,128)(2,1)S(1)} %bitcast.268), channel_id=1, source_target_pairs={{0,128},{128,0},{1,129},{129,1},{2,130},{130,2},{3,131},{131,3},{4... | collective-permute-start | bytes 4718600 | tf_op jit(solution)/shard_map/ppermute | solution.py:185
  12.3 3.2 collective-permute-start
  18.6 148.6 %all-reduce.3.cloned.1.call-start = ((), (), s32[]{:S(2)}) async-start(), calls=%async_computation.5 | async-start | bytes 1048576 | tf_op jit(solution)/shard_map/psum | solution.py:111
  18.6 97.9 %collective-permute-start.2 = (bf16[256,1024]{1,0:T(8,128)(2,1)S(1)}, bf16[256,1024]{1,0:T(8,128)(2,1)S(1)}, u32[]{:S(2)}, u32[]{:S(2)}) collective-permute-start(bf16[256,1024]{1,0:T(8,128)(2,1)S(1)} %bitcast.267), channel_id=1, source_target_pairs={{0,128},{128,0},{1,129},{129,1},{2,130},{130,2},{3,131},{131,3},{4... | collective-permute-start | bytes 1572872 | tf_op jit(solution)/shard_map/ppermute | solution.py:185
  116.6 51.8 %copy-start.8 = (bf16[256,1024]{1,0:T(8,128)(2,1)}, bf16[256,1024]{1,0:T(8,128)(2,1)S(1)}, u32[]{:S(2)}) copy-start(bf16[256,1024]{1,0:T(8,128)(2,1)S(1)} %collective-permute-done.2) | copy-start | bytes 1572868
  118.0 51.5 %copy-start.12 = (s32[128,320]{0,1:T(8,128)}, s32[128,320]{0,1:T(8,128)S(1)}, u32[]{:S(2)}) copy-start(s32[128,320]{0,1:T(8,128)S(1)} %convert_reduce_fusion.2) | copy-start | bytes 491524
  171.4 44.8 %all-to-all-start = ((bf16[32,1,20,1024]{3,2,1,0:T(8,128)(2,1)}), bf16[32,1,20,1024]{3,2,1,0:T(8,128)(2,1)S(1)}, u32[]{:S(2)}, u32[]{:S(2)}) async-start(bf16[32,1,20,1024]{3,2,1,0:T(8,128)(2,1)} %bitcast.29), calls=%async_computation | async-start | bytes 3145728 | tf_op jit(solution)/shard_map/all_to_all | solution.py:135
  181.1 6.4 %collective-permute-start.5 = (bf16[1,1024,2,352]{1,3,2,0:T(8,128)(2,1)}, bf16[1,1024,2,352]{1,3,2,0:T(8,128)(2,1)}, u32[]{:S(2)}, u32[]{:S(2)}) collective-permute-start(bf16[1,1024,2,352]{1,3,2,0:T(8,128)(2,1)} %bitcast.289), channel_id=1, source_target_pairs={{0,128},{128,0},{1,129},{129,1},{2,130},{130,2},{3,131},{131,3},{4... | collective-permute-start | bytes 4325384 | tf_op jit(solution)/shard_map/ppermute | solution.py:185
  184.4 35.4 %collective-permute-start.4 = (bf16[1,352,1024]{2,1,0:T(8,128)(2,1)S(1)}, bf16[1,352,1024]{2,1,0:T(8,128)(2,1)}, u32[]{:S(2)}, u32[]{:S(2)}) collective-permute-start(bf16[1,352,1024]{2,1,0:T(8,128)(2,1)S(1)} %bitcast.290), channel_id=1, source_target_pairs={{0,128},{128,0},{1,129},{129,1},{2,130},{130,2},{3,131},{131,3},{4... | collective-permute-start | bytes 2162696 | tf_op jit(solution)/shard_map/ppermute | solution.py:185
  223.8 43.4 %all-to-all-start.1 = ((bf16[32,1,20,1024]{3,2,1,0:T(8,128)(2,1)}), bf16[32,1,20,1024]{3,2,1,0:T(8,128)(2,1)S(1)}, u32[]{:S(2)}, u32[]{:S(2)}) async-start(bf16[32,1,20,1024]{3,2,1,0:T(8,128)(2,1)} %copy.59), calls=%async_computation.1 | async-start | bytes 3145728 | tf_op jit(solution)/shard_map/all_to_all | solution.py:140
  231.3 72.6 %all-gather.11.cloned.1.call-start = ((), (), s32[]{:S(2)}) async-start(), calls=%async_computation.8 | async-start | bytes 2621440 | tf_op jit(solution)/shard_map/all_gather | solution.py:155
  231.3 2.8 collective-permute-start.3
  269.8 119.4 %all-gather.9.cloned.1.call-start = ((), (), s32[]{:S(2)}) async-start(), calls=%async_computation.6 | async-start | bytes 4325376 | tf_op jit(solution)/shard_map/all_gather | solution.py:87
  307.5 149.6 %all-reduce.5.cloned.1.call-start = ((), (), s32[]{:S(2)}) async-start(), calls=%async_computation.7 | async-start | bytes 1048576 | tf_op jit(solution)/shard_map/psum | solution.py:111
  406.4 53.0 %copy-start.13 = (s32[128,320]{0,1:T(8,128)S(1)}, s32[128,320]{0,1:T(8,128)}, u32[]{:S(2)}) copy-start(s32[128,320]{0,1:T(8,128)} %copy-done.12) | copy-start | bytes 491524
  460.1 45.7 %copy-start.18 = (bf16[1,1,1024,2,352]{2,4,3,1,0:T(8,128)(2,1)S(1)}, bf16[1,1,1024,2,352]{2,4,3,1,0:T(8,128)(2,1)}, u32[]{:S(2)}) copy-start(bf16[1,1,1024,2,352]{2,4,3,1,0:T(8,128)(2,1)} %param.24) | copy-start | bytes 4325380
  510.6 38.2 %all-to-all-start.3 = ((bf16[32,1,20,1024]{3,2,1,0:T(8,128)(2,1)}), bf16[32,1,20,1024]{3,2,1,0:T(8,128)(2,1)S(1)}, u32[]{:S(2)}, u32[]{:S(2)}) async-start(bf16[32,1,20,1024]{3,2,1,0:T(8,128)(2,1)} %copy.64), calls=%async_computation.3 | async-start | bytes 3145728 | tf_op jit(solution)/shard_map/all_to_all | solution.py:140
  516.7 73.0 %all-gather.13.cloned.1.call-start = ((), (), s32[]{:S(2)}) async-start(), calls=%async_computation.9 | async-start | bytes 2621440 | tf_op jit(solution)/shard_map/all_gather | solution.py:155
  551.5 40.1 %copy-start.2 = (f32[128,1024]{1,0:T(8,128)S(1)}, f32[128,1024]{1,0:T(8,128)}, u32[]{:S(2)}) copy-start(f32[128,1024]{1,0:T(8,128)} %all-reduce.5.cloned.1.call-done) | copy-start | bytes 1572868
  553.9 41.5 %collective-permute-start.8 = (bf16[1,128,2,256]{1,3,2,0:T(8,128)(2,1)S(1)}, bf16[1,128,2,256]{1,3,2,0:T(8,128)(2,1)S(1)}, u32[]{:S(2)}, u32[]{:S(2)}) collective-permute-start(bf16[1,128,2,256]{1,3,2,0:T(8,128)(2,1)S(1)} %get-tuple-element.462), channel_id=1, source_target_pairs={{128,0},{129,1},{130,2},{131,3},{132,4},{133,5},{134,6},{135,7},{1... | collective-permute-start | bytes 393224 | tf_op jit(solution)/shard_map/ppermute | solution.py:201
  563.7 34.5 %collective-permute-start.6 = (bf16[128,1024]{1,0:T(8,128)(2,1)S(1)}, bf16[128,1024]{1,0:T(8,128)(2,1)S(1)}, u32[]{:S(2)}, u32[]{:S(2)}) collective-permute-start(bf16[128,1024]{1,0:T(8,128)(2,1)S(1)} %get-tuple-element.448), channel_id=1, source_target_pairs={{128,0},{129,1},{130,2},{131,3},{132,4},{133,5},{134,6},{135,7},{1... | collective-permute-start | bytes 786440 | tf_op jit(solution)/shard_map/ppermute | solution.py:200
  591.7 6.6 %collective-permute-start.7 = (bf16[128,1024]{1,0:T(8,128)(2,1)S(1)}, bf16[128,1024]{1,0:T(8,128)(2,1)S(1)}, u32[]{:S(2)}, u32[]{:S(2)}) collective-permute-start(bf16[128,1024]{1,0:T(8,128)(2,1)S(1)} %add_convert_fusion), channel_id=1, source_target_pairs={{0,128},{1,129},{2,130},{3,131},{4,132},{5,133},{6,134},{7,135},{8... | collective-permute-start | bytes 786440 | tf_op jit(solution)/shard_map/ppermute | solution.py:202
  594.0 3.3 collective-permute-start.9
  (16 other events, 177.0 us)
Sparse Core Ops, SparseCore 0:
  18.7 80.6 all-gather.6
  117.8 49.3 all-reduce.2
  270.0 33.8 all-gather.10
  307.6 81.5 all-gather.8
  407.7 49.3 all-reduce.4
  551.6 38.0 all-gather.12
